TPU v7x, 512 devices: a whole 4x8x8 slice. The times are simulated.
512 devices in a mesh: ctx: 64 (over y_lo, z, core), tp: 8 (over y_hi, x).
Axes of the slice: x: 4, y: 8 (y_hi: 2, y_lo: 4; y = y_hi * 4 + y_lo), z: 8, core: 2. Of those that a mesh axis runs over, the one named last changes fastest.
Arguments:
- tokens: bfloat16 [16384, 2048], P('ctx', 'tp'), may hold values from -6 to 6
- w_in: bfloat16 [2048, 4096], P('ctx', 'tp'), may hold values from -0.125 to 0.125
- w_bc: bfloat16 [2048, 2048], P('ctx', 'tp'), may hold values from -0.01171875 to 0.01171875
- w_dt: bfloat16 [2048, 64], P('ctx', 'tp'), may hold values from -0.125 to 0.125
- dt_bias: float32 [64], P('tp'), may hold values from -2 to 0
- decay_rate: float32 [64], P('tp'), may hold values from 1e-05 to 0.1
- skip_gain: float32 [64], P('tp'), may hold values from 0.5 to 1.5
- w_out: bfloat16 [4096, 2048], P('tp', 'ctx'), may hold values from -0.09375 to 0.09375
- cotangent: bfloat16 [16384, 2048], P('ctx', 'tp'), may hold values from -6 to 6
Outputs:
- output: bfloat16 [16384, 2048], P('ctx', 'tp')
- grad: bfloat16 [16384, 2048], P('ctx', 'tp')
All inputs are finite; a program needn't handle non-finite values.
Results may differ from a plain program's by a relative error of at most 0.0061.
Values may be sent and summed in bfloat16 or wider, within the bound.
No kernel may reach another device: no remote copies, remote signals or barrier semaphores. Data moves between devices by JAX's collectives and lax.ppermute only.
A program may use at most 128 MiB of HBM per device.

v0:
```python
import jax
import jax.numpy as jnp
from jax import lax
from jax.sharding import PartitionSpec as P

HEADDIM = 64
STATE = 128
SPAN = 256
HIGH = lax.Precision.HIGHEST


def carried_in(value, axis, combine, identity, reverse):
    devices, position = (lax.axis_size(axis), lax.axis_index(axis))
    everything = jax.tree.map(lambda part: lax.all_gather(part, axis), value)
    start = jax.tree.map(
        lambda part, zero: jnp.broadcast_to(jnp.asarray(zero, part.dtype), part.shape),
        value,
        identity,
    )

    def step(k, before):
        at = devices - 1 - k if reverse else k
        reached = at > position if reverse else at < position
        new = combine(before, jax.tree.map(lambda part: part[at], everything))
        return jax.tree.map(lambda a, b: jnp.where(reached, a, b), new, before)

    return lax.fori_loop(0, devices, step, start)


def ssd_core(values, b_rows, c_rows, step_size, decay_rate, state):
    length, heads, head_dim = values.shape
    groups = b_rows.shape[1]
    per_group = heads // groups
    blocks = length // SPAN
    lower_mask = (jnp.arange(SPAN)[:, None] >= jnp.arange(SPAN)[None, :])[None]

    def blocked(array):
        return array.reshape((blocks, SPAN) + array.shape[1:])

    def ssd_advance(carry, item):
        value_blk, b_blk, c_blk, step_blk = item
        cums = jnp.cumsum(-step_blk * decay_rate[None, :], axis=0)
        diff = cums.T[:, :, None] - cums.T[:, None, :]
        weight = jnp.where(lower_mask, jnp.exp(jnp.where(lower_mask, diff, 0.0)), 0.0)
        scores = jnp.einsum("tgn,sgn->gts", c_blk, b_blk, precision=HIGH)
        scores = jnp.repeat(scores, per_group, axis=0)
        inputs = step_blk[:, :, None] * value_blk
        inside = jnp.einsum("hts,shp->thp", scores * weight, inputs, precision=HIGH)
        c_head = jnp.repeat(c_blk, per_group, axis=1)
        b_head = jnp.repeat(b_blk, per_group, axis=1)
        carried = jnp.exp(cums)[:, :, None] * jnp.einsum(
            "thn,hpn->thp", c_head, carry, precision=HIGH
        )
        tail = jnp.exp(cums[-1][None, :] - cums)
        fresh = jnp.einsum("shp,shn->hpn", tail[:, :, None] * inputs, b_head, precision=HIGH)
        carry = jnp.exp(cums[-1])[:, None, None] * carry + fresh
        return (carry, inside + carried)

    final, outputs = lax.scan(
        jax.checkpoint(ssd_advance),
        state,
        (blocked(values), blocked(b_rows), blocked(c_rows), blocked(step_size)),
    )
    return (outputs.reshape(length, heads, head_dim), final)


def local_states(values, b_rows, step_size, decay_rate):
    length, heads, head_dim = values.shape
    groups = b_rows.shape[1]
    per_group = heads // groups
    blocks = length // SPAN

    def blocked(array):
        return array.reshape((blocks, SPAN) + array.shape[1:])

    def local_advance(carry, item):
        value_blk, b_blk, step_blk = item
        cums = jnp.cumsum(-step_blk * decay_rate[None, :], axis=0)
        tail = jnp.exp(cums[-1][None, :] - cums)
        b_head = jnp.repeat(b_blk, per_group, axis=1)
        inputs = (tail * step_blk)[:, :, None] * value_blk
        fresh = jnp.einsum("shp,shn->hpn", inputs, b_head, precision=HIGH)
        return (jnp.exp(cums[-1])[:, None, None] * carry + fresh, None)

    start = jnp.zeros((heads, head_dim, STATE), jnp.float32)
    final, unused = lax.scan(
        local_advance, start, (blocked(values), blocked(b_rows), blocked(step_size))
    )
    return final


def local_adjoint(d_mixed, c_rows, step_size, decay_rate):
    length, heads, head_dim = d_mixed.shape
    groups = c_rows.shape[1]
    per_group = heads // groups
    blocks = length // SPAN

    def blocked(array):
        return array.reshape((blocks, SPAN) + array.shape[1:])

    def retreat(carry, item):
        grad_blk, c_blk, step_blk = item
        cums = jnp.cumsum(-step_blk * decay_rate[None, :], axis=0)
        c_head = jnp.repeat(c_blk, per_group, axis=1)
        weighted = jnp.exp(cums)[:, :, None] * grad_blk
        term = jnp.einsum("thp,thn->hpn", weighted, c_head, precision=HIGH)
        return (term + jnp.exp(cums[-1])[:, None, None] * carry, None)

    start = jnp.zeros((heads, head_dim, STATE), jnp.float32)
    final, unused = lax.scan(
        retreat, start, (blocked(d_mixed), blocked(c_rows), blocked(step_size)), reverse=True
    )
    return final


def chain_combine(earlier, later):
    return (earlier[0] * later[0], later[0][:, None, None] * earlier[1] + later[1])


def per_device(tokens, w_in, w_bc, w_dt, dt_bias, decay_rate, skip_gain, w_out, cotangent):
    full_tokens = lax.all_gather(tokens, "tp", axis=1, tiled=True)
    rows = full_tokens.shape[0]
    heads = decay_rate.shape[0]
    inner = w_in.shape[1]
    pair_cols = w_bc.shape[1]
    groups = pair_cols // (2 * STATE)
    w_cat = jnp.concatenate([w_in, w_bc, w_dt], axis=1)
    whole_in, whole_out = (
        lax.all_gather(w_cat, "ctx", axis=0, tiled=True),
        lax.all_gather(w_out, "ctx", axis=1, tiled=True),
    )
    projected = jnp.dot(full_tokens, whole_in, preferred_element_type=jnp.float32)
    values = projected[:, :inner].astype(jnp.bfloat16)
    pairs = projected[:, inner : inner + pair_cols].astype(jnp.bfloat16)
    pre_step = projected[:, inner + pair_cols :] + dt_bias[None, :]
    step_size = jax.nn.softplus(pre_step)
    value_f = values.astype(jnp.float32).reshape(rows, heads, HEADDIM)
    paired = pairs.astype(jnp.float32).reshape(rows, groups, 2, STATE)
    b_rows = paired[:, :, 0]
    c_rows = paired[:, :, 1]
    zero_state = jnp.zeros((heads, HEADDIM, STATE), jnp.float32)
    end_state = local_states(value_f, b_rows, step_size, decay_rate)
    decay_total = jnp.exp(-jnp.sum(step_size * decay_rate[None, :], axis=0))
    unit_decay = jnp.ones_like(decay_total)
    state_in = carried_in(
        (decay_total, end_state), "ctx", chain_combine, (unit_decay, zero_state), False
    )[1]

    def with_state(vals, brows, crows, steps):
        return ssd_core(vals, brows, crows, steps, decay_rate, state_in)

    (core_out, core_end), pullback = jax.vjp(with_state, value_f, b_rows, c_rows, step_size)
    mixed = (
        (core_out + skip_gain[None, :, None] * value_f).reshape(rows, inner).astype(jnp.bfloat16)
    )
    partial_out = jnp.dot(mixed, whole_out, preferred_element_type=jnp.float32)
    output = lax.psum_scatter(partial_out, "tp", scatter_dimension=1, tiled=True).astype(
        jnp.bfloat16
    )
    full_cotangent = lax.all_gather(cotangent, "tp", axis=1, tiled=True)
    d_flat = lax.dot_general(
        full_cotangent, whole_out, (((1,), (1,)), ((), ())), preferred_element_type=jnp.float32
    )
    d_mixed = d_flat.reshape(rows, heads, HEADDIM)
    own_adjoint = local_adjoint(d_mixed, c_rows, step_size, decay_rate)
    adjoint = carried_in(
        (decay_total, own_adjoint), "ctx", chain_combine, (unit_decay, zero_state), True
    )[1]
    grads = pullback((d_mixed, adjoint))
    d_values = grads[0] + skip_gain[None, :, None] * d_mixed
    d_pre = grads[3] * jax.nn.sigmoid(pre_step)
    d_pairs = jnp.stack([grads[1], grads[2]], axis=2).reshape(rows, pair_cols)
    d_cat = jnp.concatenate(
        [
            d_values.reshape(rows, inner).astype(jnp.bfloat16),
            d_pairs.astype(jnp.bfloat16),
            d_pre.astype(jnp.bfloat16),
        ],
        axis=1,
    )
    partial_grad = lax.dot_general(
        d_cat, whole_in, (((1,), (1,)), ((), ())), preferred_element_type=jnp.float32
    )
    grad = lax.psum_scatter(partial_grad, "tp", scatter_dimension=1, tiled=True).astype(
        jnp.bfloat16
    )
    return (output, grad)


def solution(mesh):
    placed = (
        P("ctx", "tp"),
        P("ctx", "tp"),
        P("ctx", "tp"),
        P("ctx", "tp"),
        P("tp"),
        P("tp"),
        P("tp"),
        P("tp", "ctx"),
        P("ctx", "tp"),
    )
    return jax.shard_map(
        per_device,
        mesh=mesh,
        in_specs=placed,
        out_specs=(P("ctx", "tp"), P("ctx", "tp")),
        check_vma=False,
    )
```

profile of v0, /device:TPU:8, one launch (start us, length us, event | category | flops | bytes accessed | tf_op | source)
XLA Modules:
  0.0 956.6 jit_solution(10502070990085466387)
XLA Ops:
  8.7 1.4 pad_maximum_fusion.1
  11.5 70.3 %all-gather.12.cloned.1.call-done = bf16[256,2048]{1,0:T(8,128)(2,1)} async-done(((bf16[256,256]{1,0:T(8,128)(2,1)}), bf16[256,2048]{1,0:T(8,128)(2,1)}) %all-gather.12.cloned.1.call-update) | async-done | bytes 1048592 | tf_op jit(solution)/shard_map/all_gather | solution.py:121
  81.9 118.4 %all-gather.10.cloned.1.call-done = bf16[2048,776]{1,0:T(8,128)(2,1)} async-done(((bf16[32,776]{1,0:T(8,128)(2,1)}), bf16[2048,776]{1,0:T(8,128)(2,1)}) %all-gather.10.cloned.1.call-update) | async-done | bytes 3178512 | tf_op jit(solution)/shard_map/all_gather | solution.py:129
  200.3 3.5 fusion.87
  206.0 1.3 convolution_add_fusion.1
  207.4 61.4 %all-gather.16.cloned.1.call-done = bf16[256,2048]{1,0:T(8,128)(2,1)} async-done(((bf16[256,256]{1,0:T(8,128)(2,1)}), bf16[256,2048]{1,0:T(8,128)(2,1)}) %all-gather.16.cloned.1.call-update) | async-done | bytes 1048592 | tf_op jit(solution)/shard_map/all_gather | solution.py:160
  268.9 115.9 %all-gather.14.cloned.1.call-done = bf16[512,2048]{0,1:T(8,128)(2,1)} async-done(((bf16[512,32]{0,1:T(8,128)(2,1)}), bf16[512,2048]{0,1:T(8,128)(2,1)}) %all-gather.14.cloned.1.call-update) | async-done | bytes 2097168 | tf_op jit(solution)/shard_map/all_gather | solution.py:130
  384.7 2.8 fusion.89
  387.7 1.4 convolution_add_fusion
  389.9 1.3 dynamic-slice.2
  392.0 107.6 %all-reduce.2 = f32[512]{0:T(512)S(1)} all-reduce(f32[512]{0:T(512)S(1)} %exponential_dynamic-update-slice_fusion), channel_id=2, replica_groups=mesh['ctx'=64,'tp'=8] {'ctx'}, use_global_device_ids=true, to_apply=%add.2 | all-reduce | flops 512 | bytes 4096
  500.0 2.5 fusion.12
  502.5 16.9 %all-gather.18.cloned.1.call-done = f32[512,64,128]{2,1,0:T(8,128)} async-done(((f32[8,64,128]{2,1,0:T(8,128)}), f32[512,64,128]{2,1,0:T(8,128)}) %all-gather.18.cloned.1.call-update) | async-done | bytes 16777232 | tf_op jit(solution)/shard_map/all_gather | solution.py:14
  519.5 70.3 %while.22 = (s32[]{:T(128)}, f32[8,64,128]{2,1,0:T(8,128)S(1)}, s32[]{:T(128)}, f32[64,8]{1,0:T(8,128)S(1)}, f32[64,8,64,128]{3,2,1,0:T(8,128)}, /*index=5*/s32[]{:T(128)}, s32[]{:T(128)}) while((s32[]{:T(128)}, f32[8,64,128]{2,1,0:T(8,128)S(1)}, s32[]{:T(128)}, f32[64,8]{1,0:T(8,128)S(1)}, f32[64,8,64,128]{3,2,1,0:T(8,128)}, ...), condition=%wide.region_4.5_spmd.clone, body=%wide.region_3.4_spmd.clone.sunk | while | flops 262148 | bytes 786633 | solution.py:27
  535.9 1.1 fusion.106
  540.3 1.1 fusion.106
  541.4 1.1 fusion.106
  542.5 1.1 fusion.106
  544.7 1.1 fusion.106
  549.1 1.1 fusion.106
  551.3 1.1 fusion.106
  552.4 1.1 fusion.106
  557.9 1.1 fusion.106
  559.0 1.1 fusion.106
  560.1 1.1 fusion.106
  562.3 1.1 fusion.106
  565.6 1.1 fusion.106
  567.8 1.1 fusion.106
  571.1 1.1 fusion.106
  576.6 1.1 fusion.106
  577.7 1.1 fusion.106
  583.2 1.1 fusion.106
  584.3 1.1 fusion.106
  589.7 66.3 %all-gather.20.cloned.1.call-done = f32[512,64,128]{2,1,0:T(8,128)} async-done(((f32[8,64,128]{2,1,0:T(8,128)}), f32[512,64,128]{2,1,0:T(8,128)}) %all-gather.20.cloned.1.call-update) | async-done | bytes 16777232 | tf_op jit(solution)/shard_map/all_gather | solution.py:14
  656.1 70.8 %while.23 = (s32[]{:T(128)}, f32[8,64,128]{2,1,0:T(8,128)S(1)}, s32[]{:T(128)}, f32[64,8]{1,0:T(8,128)S(1)}, f32[64,8,64,128]{3,2,1,0:T(8,128)}, /*index=5*/s32[]{:T(128)}, s32[]{:T(128)}, s32[]{:T(128)}, s32[]{:T(128)}) while((s32[]{:T(128)}, f32[8,64,128]{2,1,0:T(8,128)S(1)}, s32[]{:T(128)}, f32[64,8]{1,0:T(8,128)S(1)}, ...), condition=%wide.region_7.8_spmd.clone, body=%wide.region_6.7_spmd.clone.sunk | while | flops 262152 | bytes 786695 | solution.py:27
  730.0 3.1 fusion.22
  733.9 1.2 convolution_bitcast_fusion.2
  735.1 3.4 multiply_reduce_fusion.1
  738.9 1.2 fusion.26
  740.2 2.7 reduce-window.44
  743.0 1.2 fusion.20
  745.3 2.7 fusion.59
  748.0 1.5 copy-done.1
  749.5 2.1 fusion.88
  751.6 95.5 %reduce-scatter.5.cloned.1.call-done = f32[256,256]{1,0:T(8,128)} async-done(((f32[256,2048]{1,0:T(8,128)}), f32[256,256]{1,0:T(8,128)}) %reduce-scatter.5.cloned.1.call-update) | async-done | bytes 262160 | tf_op jit(solution)/shard_map/reduce_scatter | solution.py:184
  847.1 1.6 convert_element_type.31
  848.7 99.5 %reduce-scatter.3.cloned.1.call-done = f32[256,256]{1,0:T(8,128)} async-done(((f32[256,2048]{1,0:T(8,128)}), f32[256,256]{1,0:T(8,128)}) %reduce-scatter.3.cloned.1.call-update) | async-done | bytes 262160 | tf_op jit(solution)/shard_map/reduce_scatter | solution.py:157
  948.1 1.6 convert_element_type.27
  (327 shorter events, 128.3 us)
Async XLA Ops:
  7.2 74.7 %all-gather.12.cloned.1.call-start = ((), (), s32[]{:S(2)}) async-start(), calls=%async_computation.3 | async-start | bytes 1179648 | tf_op jit(solution)/shard_map/all_gather | solution.py:121
  7.9 192.4 %all-gather.10.cloned.1.call-start = ((), (), s32[]{:S(2)}) async-start(), calls=%async_computation.2 | async-start | bytes 3727360 | tf_op jit(solution)/shard_map/all_gather | solution.py:129
  10.1 258.7 %all-gather.16.cloned.1.call-start = ((), (), s32[]{:S(2)}) async-start(), calls=%async_computation.6 | async-start | bytes 1179648 | tf_op jit(solution)/shard_map/all_gather | solution.py:160
  10.9 373.9 %all-gather.14.cloned.1.call-start = ((), (), s32[]{:S(2)}) async-start(), calls=%async_computation.4 | async-start | bytes 2129920 | tf_op jit(solution)/shard_map/all_gather | solution.py:130
  11.5 192.3 %copy-start.3 = (f32[8]{0:T(128)S(1)}, f32[8]{0:T(128)}, u32[]{:S(2)}) copy-start(f32[8]{0:T(128)} %param.18) | copy-start | bytes 100
  11.5 192.3 %copy-start.6 = (f32[8]{0:T(128)S(1)}, f32[8]{0:T(128)}, u32[]{:S(2)}) copy-start(f32[8]{0:T(128)} %param.17) | copy-start | bytes 100
  11.5 508.0 %all-gather.18.cloned.1.call-start = ((), (), s32[]{:S(2)}) async-start(), calls=%async_computation.8 | async-start | bytes 17039360 | tf_op jit(solution)/shard_map/all_gather | solution.py:14
  203.7 0.9 copy-start.9
  207.4 181.8 %copy-start.8 = (f32[8]{0:T(128)S(1)}, f32[8]{0:T(128)}, u32[]{:S(2)}) copy-start(f32[8]{0:T(128)} %param.19) | copy-start | bytes 100
  207.4 448.7 %all-gather.20.cloned.1.call-start = ((), (), s32[]{:S(2)}) async-start(), calls=%async_computation.9 | async-start | bytes 17039360 | tf_op jit(solution)/shard_map/all_gather | solution.py:14
  389.1 458.0 %reduce-scatter.5.cloned.1.call-start = ((), (), s32[]{:S(2)}) async-start(), calls=%async_computation.7 | async-start | bytes 2359296 | tf_op jit(solution)/shard_map/reduce_scatter | solution.py:184
  738.5 5.7 copy-start.4
  738.5 5.7 copy-start.7
  738.5 6.5 copy-start.5
  738.9 6.2 copy-start.2
  743.0 2.2 copy-start
  747.9 1.6 copy-start.1
  748.0 200.2 %reduce-scatter.3.cloned.1.call-start = ((), (), s32[]{:S(2)}) async-start(), calls=%async_computation.5 | async-start | bytes 2359296 | tf_op jit(solution)/shard_map/reduce_scatter | solution.py:157
Sparse Core Ops, SparseCore 0:
  11.1 70.7 all-gather.11
  84.6 115.6 all-gather.9
  203.3 65.5 all-gather.15
  270.9 113.8 all-gather.13
  386.7 132.6 all-gather.17
  521.5 134.5 all-gather.19
  748.1 98.9 reduce-scatter.4
  852.4 95.7 reduce-scatter.2
where the time goes:
time: 961 us; the launch traced here: 957 us
  waiting for transfers between devices  646 us (67%)
  other arithmetic  146 us (15%)
  blocking collectives  108 us (11%)
  matrix products  28.9 us (3%)
  between operations  15.1 us (2%)
    select_n x128, other arithmetic, step(): return jax.tree.map(lambda a, b: jnp.where(reached, a, b), new, before)  135 us
    all_gather x1, waiting for transfers between devices, per_device(): lax.all_gather(w_cat, 'ctx', axis=0, tiled=True)  118 us
    all_gather x1, waiting for transfers between devices, per_device(): lax.all_gather(w_out, 'ctx', axis=1, tiled=True)  116 us
    unnamed x1, blocking collectives  108 us
    reduce_scatter x1, waiting for transfers between devices, per_device(): lax.psum_scatter(partial_out, 'tp', scatter_dimension=1, tiled=True)  99.5 us
    reduce_scatter x1, waiting for transfers between devices, per_device(): lax.psum_scatter(partial_grad, 'tp', scatter_dimension=1, tiled=True)  95.5 us
    all_gather x2, waiting for transfers between devices, carried_in(): everything = jax.tree.map(lambda part: lax.all_gather(part, axis), value)  83.3 us
    all_gather x1, waiting for transfers between devices, per_device(): full_tokens = lax.all_gather(tokens, 'tp', axis=1, tiled=True)  70.3 us
  transfers between devices with their start and end apart: 8, of which 8 were waited for; matrix products, arithmetic and copies ran while one was open for 9% of the time, Pallas kernels for 0%

commit v1 on v0

--- a/solution.py
+++ b/solution.py
@@ -118,7 +118,9 @@
 
 
 def per_device(tokens, w_in, w_bc, w_dt, dt_bias, decay_rate, skip_gain, w_out, cotangent):
-    full_tokens = lax.all_gather(tokens, "tp", axis=1, tiled=True)
+    full_tokens = jnp.concatenate(
+        lax.all_to_all(jnp.stack([tokens] * lax.axis_size("tp")), "tp", 0, 0), axis=1
+    )
     rows = full_tokens.shape[0]
     heads = decay_rate.shape[0]
     inner = w_in.shape[1]

time: 961 us -> 908 us (0.945)
  waiting for transfers between devices: 646 us -> 583 us
    all_gather x1 -> x0, waiting for transfers between devices: 70.3 us -> none  [per_device(): full_tokens = lax.all_gather(tokens, 'tp', axis=1, tiled=True)]
    all_to_all x0 -> x1, waiting for transfers between devices: none -> 30.6 us  [per_device(): lax.all_to_all(jnp.stack([tokens] * lax.axis_size('tp')), 'tp', 0, 0)]
    all_gather x1, waiting for transfers between devices: 118 us -> 95.6 us  [per_device(): lax.all_gather(w_cat, 'ctx', axis=0, tiled=True)]
  transfers between devices with their start and end apart: 8 -> 8, of which waited for: 8 -> 8; matrix products, arithmetic and copies ran while one was open for 9% -> 10% of each run, Pallas kernels for 0% -> 0%
where the time goes in v1:
time: 908 us; the launch traced here: 904 us
  waiting for transfers between devices  583 us (64%)
  other arithmetic  146 us (16%)
  blocking collectives  108 us (12%)
  matrix products  28.6 us (3%)
  between operations  15.1 us (2%)
  local copies, waits for them, and re-layouts  9.57 us (1%)
    select_n x128, other arithmetic, step(): return jax.tree.map(lambda a, b: jnp.where(reached, a, b), new, before)  135 us
    all_gather x1, waiting for transfers between devices, per_device(): lax.all_gather(w_out, 'ctx', axis=1, tiled=True)  116 us
    unnamed x1, blocking collectives  108 us
    reduce_scatter x1, waiting for transfers between devices, per_device(): lax.psum_scatter(partial_out, 'tp', scatter_dimension=1, tiled=True)  99.5 us
    reduce_scatter x1, waiting for transfers between devices, per_device(): lax.psum_scatter(partial_grad, 'tp', scatter_dimension=1, tiled=True)  96.1 us
    all_gather x1, waiting for transfers between devices, per_device(): lax.all_gather(w_cat, 'ctx', axis=0, tiled=True)  95.6 us
    all_gather x2, waiting for transfers between devices, carried_in(): everything = jax.tree.map(lambda part: lax.all_gather(part, axis), value)  83.6 us
    all_gather x1, waiting for transfers between devices, per_device(): full_cotangent = lax.all_gather(cotangent, 'tp', axis=1, tiled=True)  60.1 us
  transfers between devices with their start and end apart: 8, of which 8 were waited for; matrix products, arithmetic and copies ran while one was open for 10% of the time, Pallas kernels for 0%

profile of v1, /device:TPU:8, one launch (start us, length us, event | category | flops | bytes accessed | tf_op | source)
XLA Modules:
  0.0 903.7 jit_solution(7668827267790254160)
XLA Ops:
  8.0 1.4 pad_maximum_fusion.1
  11.2 1.1 stack.5
  12.3 8.7 all-to-all-start
  21.7 30.6 %all-to-all-done = bf16[8,256,256]{1,2,0:T(8,128)(2,1)S(1)} async-done(((bf16[8,256,256]{1,2,0:T(8,128)(2,1)}), bf16[8,256,256]{1,2,0:T(8,128)(2,1)S(1)}, u32[]{:S(2)}, u32[]{:S(2)}) %all-to-all-start) | async-done | bytes 1048608 | tf_op jit(solution)/shard_map/all_to_all | solution.py:122
  52.3 95.6 %all-gather.9.cloned.1.call-done = bf16[2048,776]{1,0:T(8,128)(2,1)} async-done(((bf16[32,776]{1,0:T(8,128)(2,1)}), bf16[2048,776]{1,0:T(8,128)(2,1)}) %all-gather.9.cloned.1.call-update) | async-done | bytes 3178512 | tf_op jit(solution)/shard_map/all_gather | solution.py:131
  147.9 3.2 fusion.87
  153.4 1.3 convolution_add_fusion.1
  154.8 60.1 %all-gather.13.cloned.1.call-done = bf16[256,2048]{1,0:T(8,128)(2,1)} async-done(((bf16[256,256]{1,0:T(8,128)(2,1)}), bf16[256,2048]{1,0:T(8,128)(2,1)}) %all-gather.13.cloned.1.call-update) | async-done | bytes 1048592 | tf_op jit(solution)/shard_map/all_gather | solution.py:162
  214.9 116.0 %all-gather.11.cloned.1.call-done = bf16[512,2048]{0,1:T(8,128)(2,1)} async-done(((bf16[512,32]{0,1:T(8,128)(2,1)}), bf16[512,2048]{0,1:T(8,128)(2,1)}) %all-gather.11.cloned.1.call-update) | async-done | bytes 2097168 | tf_op jit(solution)/shard_map/all_gather | solution.py:132
  330.9 2.8 fusion.89
  333.9 1.4 convolution_add_fusion
  336.1 1.3 dynamic-slice.2
  338.2 107.6 %all-reduce.2 = f32[512]{0:T(512)S(1)} all-reduce(f32[512]{0:T(512)S(1)} %exponential_dynamic-update-slice_fusion), channel_id=2, replica_groups=mesh['ctx'=64,'tp'=8] {'ctx'}, use_global_device_ids=true, to_apply=%add.2 | all-reduce | flops 512 | bytes 4096
  446.2 2.5 fusion.12
  448.7 17.4 %all-gather.15.cloned.1.call-done = f32[512,64,128]{2,1,0:T(8,128)} async-done(((f32[8,64,128]{2,1,0:T(8,128)}), f32[512,64,128]{2,1,0:T(8,128)}) %all-gather.15.cloned.1.call-update) | async-done | bytes 16777232 | tf_op jit(solution)/shard_map/all_gather | solution.py:14
  466.2 70.1 %while.22 = (s32[]{:T(128)}, f32[8,64,128]{2,1,0:T(8,128)S(1)}, s32[]{:T(128)}, f32[64,8]{1,0:T(8,128)S(1)}, f32[64,8,64,128]{3,2,1,0:T(8,128)}, /*index=5*/s32[]{:T(128)}, s32[]{:T(128)}) while((s32[]{:T(128)}, f32[8,64,128]{2,1,0:T(8,128)S(1)}, s32[]{:T(128)}, f32[64,8]{1,0:T(8,128)S(1)}, f32[64,8,64,128]{3,2,1,0:T(8,128)}, ...), condition=%wide.region_4.5_spmd.clone, body=%wide.region_3.4_spmd.clone.sunk | while | flops 262148 | bytes 786633 | solution.py:27
  485.8 1.1 fusion.106
  489.1 1.1 fusion.106
  491.3 1.1 fusion.106
  494.6 1.1 fusion.106
  499.0 1.1 fusion.106
  506.7 1.1 fusion.106
  512.2 1.1 fusion.106
  514.3 1.1 fusion.106
  515.4 1.1 fusion.106
  516.5 1.1 fusion.106
  519.8 1.1 fusion.106
  522.0 1.1 fusion.106
  523.1 1.1 fusion.106
  528.6 1.1 fusion.106
  529.7 1.1 fusion.106
  532.0 1.1 fusion.106
  536.3 66.2 %all-gather.17.cloned.1.call-done = f32[512,64,128]{2,1,0:T(8,128)} async-done(((f32[8,64,128]{2,1,0:T(8,128)}), f32[512,64,128]{2,1,0:T(8,128)}) %all-gather.17.cloned.1.call-update) | async-done | bytes 16777232 | tf_op jit(solution)/shard_map/all_gather | solution.py:14
  602.5 70.8 %while.23 = (s32[]{:T(128)}, f32[8,64,128]{2,1,0:T(8,128)S(1)}, s32[]{:T(128)}, f32[64,8]{1,0:T(8,128)S(1)}, f32[64,8,64,128]{3,2,1,0:T(8,128)}, /*index=5*/s32[]{:T(128)}, s32[]{:T(128)}, s32[]{:T(128)}, s32[]{:T(128)}) while((s32[]{:T(128)}, f32[8,64,128]{2,1,0:T(8,128)S(1)}, s32[]{:T(128)}, f32[64,8]{1,0:T(8,128)S(1)}, ...), condition=%wide.region_7.8_spmd.clone, body=%wide.region_6.7_spmd.clone.sunk | while | flops 262152 | bytes 786695 | solution.py:27
  608.0 1.1 fusion.107
  676.5 3.1 fusion.22
  680.4 1.2 convolution_bitcast_fusion.2
  681.6 3.4 multiply_reduce_fusion.1
  685.3 1.2 fusion.26
  686.6 2.7 reduce-window.44
  689.5 1.2 fusion.20
  691.7 2.7 fusion.59
  694.4 1.5 copy-done.1
  695.9 2.1 fusion.88
  698.0 96.1 %reduce-scatter.5.cloned.1.call-done = f32[256,256]{1,0:T(8,128)} async-done(((f32[256,2048]{1,0:T(8,128)}), f32[256,256]{1,0:T(8,128)}) %reduce-scatter.5.cloned.1.call-update) | async-done | bytes 262160 | tf_op jit(solution)/shard_map/reduce_scatter | solution.py:186
  794.1 1.6 convert_element_type.31
  795.8 99.5 %reduce-scatter.3.cloned.1.call-done = f32[256,256]{1,0:T(8,128)} async-done(((f32[256,2048]{1,0:T(8,128)}), f32[256,256]{1,0:T(8,128)}) %reduce-scatter.3.cloned.1.call-update) | async-done | bytes 262160 | tf_op jit(solution)/shard_map/reduce_scatter | solution.py:159
  895.2 1.6 convert_element_type.27
  (328 shorter events, 130.8 us)
Async XLA Ops:
  7.2 140.7 %all-gather.9.cloned.1.call-start = ((), (), s32[]{:S(2)}) async-start(), calls=%async_computation.3 | async-start | bytes 3727360 | tf_op jit(solution)/shard_map/all_gather | solution.py:131
  9.4 205.5 %all-gather.13.cloned.1.call-start = ((), (), s32[]{:S(2)}) async-start(), calls=%async_computation.6 | async-start | bytes 1179648 | tf_op jit(solution)/shard_map/all_gather | solution.py:162
  12.3 40.0 %all-to-all-start = ((bf16[8,256,256]{1,2,0:T(8,128)(2,1)}), bf16[8,256,256]{1,2,0:T(8,128)(2,1)S(1)}, u32[]{:S(2)}, u32[]{:S(2)}) async-start(bf16[8,256,256]{1,2,0:T(8,128)(2,1)} %stack.5), calls=%async_computation | async-start | bytes 2097152 | tf_op jit(solution)/shard_map/all_to_all | solution.py:122
  20.9 310.0 %all-gather.11.cloned.1.call-start = ((), (), s32[]{:S(2)}) async-start(), calls=%async_computation.4 | async-start | bytes 2129920 | tf_op jit(solution)/shard_map/all_gather | solution.py:132
  21.7 444.5 %all-gather.15.cloned.1.call-start = ((), (), s32[]{:S(2)}) async-start(), calls=%async_computation.8 | async-start | bytes 17039360 | tf_op jit(solution)/shard_map/all_gather | solution.py:14
  147.9 3.2 copy-start.3
  147.9 3.2 copy-start.6
  151.1 0.9 copy-start.9
  154.8 180.6 %copy-start.8 = (f32[8]{0:T(128)S(1)}, f32[8]{0:T(128)}, u32[]{:S(2)}) copy-start(f32[8]{0:T(128)} %param.19) | copy-start | bytes 100
  154.8 447.7 %all-gather.17.cloned.1.call-start = ((), (), s32[]{:S(2)}) async-start(), calls=%async_computation.9 | async-start | bytes 17039360 | tf_op jit(solution)/shard_map/all_gather | solution.py:14
  335.3 458.8 %reduce-scatter.5.cloned.1.call-start = ((), (), s32[]{:S(2)}) async-start(), calls=%async_computation.7 | async-start | bytes 2359296 | tf_op jit(solution)/shard_map/reduce_scatter | solution.py:186
  684.9 5.7 copy-start.4
  684.9 5.7 copy-start.7
  684.9 6.5 copy-start.5
  685.3 6.2 copy-start.2
  689.4 2.2 copy-start
  694.3 1.6 copy-start.1
  694.4 200.9 %reduce-scatter.3.cloned.1.call-start = ((), (), s32[]{:S(2)}) async-start(), calls=%async_computation.5 | async-start | bytes 2359296 | tf_op jit(solution)/shard_map/reduce_scatter | solution.py:159
Sparse Core Ops, SparseCore 0:
  10.7 137.1 all-gather.8
  150.9 63.9 all-gather.12
  217.1 113.8 all-gather.10
  332.9 133.1 all-gather.14
  468.1 134.2 all-gather.16
  694.5 99.6 reduce-scatter.4
  799.5 95.7 reduce-scatter.2
